TPU v7x, 256 devices: a whole 4x4x8 slice. The times are simulated.
256 devices in a mesh: clu: 32 (over x, z), grp: 8 (over y, core).
Axes of the slice: x: 4, y: 4, z: 8, core: 2. Of those that a mesh axis runs over, the one named last changes fastest.
Arguments:
- tokens: bfloat16 [262144, 1024], P(('clu', 'grp')), may hold values from -6 to 6
- segment_ids: int32 [256, 1024], P(('clu', 'grp')), may hold values from 0 to 127, never falling along the last dimension, each value on 1 to 32 neighbouring positions
- w_in: bfloat16 [1024, 2048], replicated, may hold values from -0.1875 to 0.1875
- b_in: float32 [2048], replicated, may hold values from -4 to 4
- w_out: bfloat16 [2048, 1024], replicated, may hold values from -0.125 to 0.125
- b_out: float32 [1024], replicated, may hold values from -1.5 to 1.5
- owner_ids: int32 [32768, 1], P(('clu', 'grp')), may hold values from 0 to 31; in each aligned block of 128 rows (0 to 127, 128 to 255, ...) at most 8 rows name the same one
- sub_ids: int32 [32768], P(('clu', 'grp')), may hold values from 0 to 511
Outputs:
- pooled: bfloat16 [32768, 1024], P(('clu', 'grp'))
- nearest: float32 [32768], P(('clu', 'grp'))
Inputs may be any that keep to these rules, and one draw needn't show every extreme that they name: `owner_ids`: no device holds more than 8 documents of one owner; some device holds exactly 8. `segment_ids`: each row lists documents 0 to 127 in order, each on 1 to 32 consecutive positions, one on exactly 32.
All inputs are finite; a program needn't handle non-finite values.
Results may differ from a plain program's by a relative error of at most 0.0043.
Values may be sent and summed in bfloat16 or wider, within the bound.
No kernel may reach another device: no remote copies, remote signals or barrier semaphores. Data moves between devices by JAX's collectives and lax.ppermute only.
A program may use at most 64 MiB of HBM per device.

v0:
```python
import jax
import jax.numpy as jnp
from jax import lax
from jax.sharding import PartitionSpec as P


def encode(token_block, segments, w_in, b_in, w_out, b_out, doc_count):
    pre_act = jnp.dot(token_block, w_in, preferred_element_type=jnp.float32) + b_in
    activated = jax.nn.gelu(pre_act, approximate=False).astype(jnp.bfloat16)
    layer_out = (
        token_block.astype(jnp.float32)
        + jnp.dot(activated, w_out, preferred_element_type=jnp.float32)
        + b_out
    ).astype(jnp.bfloat16)
    member = segments[None, :] == jnp.arange(doc_count, dtype=jnp.int32)[:, None]
    totals = jnp.dot(member.astype(jnp.bfloat16), layer_out, preferred_element_type=jnp.float32)
    counts = jnp.sum(member.astype(jnp.float32), axis=1, keepdims=True)
    mean_rows = totals / counts
    scale_inv = lax.rsqrt(jnp.sum(mean_rows * mean_rows, axis=1, keepdims=True) + 1e-06)
    return (mean_rows.astype(jnp.bfloat16), (mean_rows * scale_inv).astype(jnp.bfloat16))


def absorb(best_sim, own_units, own_meta, piece_units, piece_meta):
    similar = lax.dot_general(
        own_units, piece_units, (((1,), (1,)), ((), ())), preferred_element_type=jnp.float32
    )
    own_key = own_meta[:, 1][:, None]
    matched = (
        (own_key == piece_meta[:, 1][None, :])
        & (own_key >= 0)
        & (own_meta[:, 0][:, None] != piece_meta[:, 0][None, :])
    )
    return jnp.maximum(best_sim, jnp.max(jnp.where(matched, similar, -1.0), axis=1))


def per_device(tokens, segment_ids, w_in, b_in, w_out, b_out, owner_ids, sub_ids):
    n_clu = lax.axis_size("clu")
    n_grp = lax.axis_size("grp")
    doc_count = owner_ids.shape[0]
    model_width = tokens.shape[1]
    capacity = 2 * doc_count // n_clu
    own_count = n_clu * capacity
    pooled, unit_rows = encode(tokens, segment_ids[0], w_in, b_in, w_out, b_out, doc_count)
    owner_rank = owner_ids[:, 0]
    owner_hits = (owner_rank[:, None] == jnp.arange(n_clu, dtype=jnp.int32)[None, :]).astype(
        jnp.int32
    )
    before = jnp.cumsum(owner_hits, axis=0) - owner_hits
    slot_index = jnp.sum(before * owner_hits, axis=1)
    slot_place = owner_rank * capacity + slot_index
    grp_index = lax.axis_index("grp")
    device_rank = lax.axis_index("clu") * n_grp + grp_index
    doc_index = device_rank * doc_count + jnp.arange(doc_count, dtype=jnp.int32)
    start_best = jnp.full((own_count,), -1.0, jnp.float32)
    doc_info = jnp.stack([slot_place, doc_index, sub_ids], axis=1)
    every_unit, every_info = (
        lax.all_gather(unit_rows, "grp", axis=0, tiled=True),
        lax.all_gather(doc_info, "grp", axis=0, tiled=True),
    )
    source_grp = jnp.arange(n_grp * doc_count, dtype=jnp.int32) // doc_count
    wide_place = (
        every_info[:, 0] // capacity * (n_grp * capacity)
        + source_grp * capacity
        + every_info[:, 0] % capacity
    )
    send_units = (
        jnp.zeros((n_clu * n_grp * capacity, model_width), jnp.bfloat16)
        .at[wide_place]
        .set(every_unit)
    )
    send_meta = (
        jnp.full((n_clu * n_grp * capacity, 2), -1, jnp.int32).at[wide_place].set(every_info[:, 1:])
    )
    got_units, got_meta = (
        lax.all_to_all(
            send_units.reshape(n_clu, n_grp * capacity, model_width),
            "clu",
            split_axis=0,
            concat_axis=0,
            tiled=True,
        ),
        lax.all_to_all(
            send_meta.reshape(n_clu, n_grp * capacity, 2),
            "clu",
            split_axis=0,
            concat_axis=0,
            tiled=True,
        ),
    )
    own_units = lax.dynamic_slice_in_dim(
        got_units.reshape(n_clu, n_grp, capacity, model_width), grp_index, 1, 1
    ).reshape(own_count, model_width)
    own_meta = lax.dynamic_slice_in_dim(
        got_meta.reshape(n_clu, n_grp, capacity, 2), grp_index, 1, 1
    ).reshape(own_count, 2)
    best_sim = absorb(
        start_best,
        own_units,
        own_meta,
        got_units.reshape(n_clu * n_grp * capacity, model_width),
        got_meta.reshape(n_clu * n_grp * capacity, 2),
    )
    returned = lax.all_to_all(
        best_sim.reshape(n_clu, capacity), "clu", split_axis=0, concat_axis=0, tiled=True
    )
    nearest = jnp.take(returned.reshape(own_count), slot_place)
    return (pooled, nearest)


def solution(mesh):
    in_specs = (
        P(("clu", "grp"), None),
        P(("clu", "grp"), None),
        P(),
        P(),
        P(),
        P(),
        P(("clu", "grp"), None),
        P(("clu", "grp")),
    )
    out_specs = (P(("clu", "grp"), None), P(("clu", "grp")))
    return jax.shard_map(
        per_device, mesh=mesh, in_specs=in_specs, out_specs=out_specs, check_vma=False
    )
```

profile of v0, /device:TPU:1, one launch (start us, length us, event | category | flops | bytes accessed | tf_op | source)
XLA Modules:
  0.0 217.7 jit_solution(3338972314123578086)
XLA Ops:
  7.2 0.8 convert_reduce_fusion
  8.1 30.1 %fusion.10 = f32[1024,1024]{1,0:T(8,128)} fusion(bf16[2048,1024]{1,0:T(8,128)(2,1)} %param.12, f32[2048]{0:T(1024)} %param.11, bf16[1024,1024]{1,0:T(8,128)(2,1)} %param.8, bf16[1024,2048]{1,0:T(8,128)(2,1)} %param.10), kind=kOutput, calls=%fused_computation.23 | convolution fusion | flops 8728346624 | bytes 14688256 | tf_op jit(solution)/shard_map/dot_general | solution.py:12
  38.2 3.1 %multiply_reduce_fusion = (f32[128]{0:T(128)S(1)}, f32[128,1024]{1,0:T(8,128)S(1)}) fusion(f32[128]{0:T(128)S(1)} %convert_reduce_fusion, f32[1024,1024]{1,0:T(8,128)} %fusion.10, bf16[1024,1024]{1,0:T(8,128)(2,1)S(1)} %copy-done, f32[1024]{0:T(1024)S(1)} %copy-done.3, s32[1024]{0:T(1024)S(1)} %bitcast.43), kind=kOutput, calls=%fused_computation.35 | convolution fusion | flops 273153920 | bytes 6824960 | tf_op jit(solution)/shard_map/dot_general | solution.py:16
  41.3 0.8 multiply_convert_fusion
  42.6 14.5 %all_gather.6 = s32[1024,3]{0,1:T(4,128)S(1)} all-gather(s32[128,3]{0,1:T(4,128)S(1)} %pad_add_fusion), channel_id=1, replica_groups=mesh['clu'=32,'grp'=8] {'grp'}, dimensions={0}, use_global_device_ids=true | all-gather | bytes 13824 | tf_op jit(solution)/shard_map/all_gather | solution.py:58
  57.2 0.2 copy.28
  57.5 3.3 %scatter_custom_fusion = s32[2048,2]{1,0:T(8,128)S(1)} fusion(s32[1024]{0:T(1024)S(1)} %bitcast.48, s32[1024,2]{1,0:T(8,128)S(1)} %copy.28, s32[]{:T(128)} %constant.133.clone.1), kind=kCustom, calls=%fused_computation.36 | custom fusion | bytes 16388 | tf_op jit(solution)/shard_map/scatter | solution.py:72
  60.8 0.4 copy.29
  61.2 0.7 reshape.157
  61.9 10.2 %all-to-all-start = ((s32[32,1,128]{2,1,0:T(1,128)}), s32[32,1,128]{2,1,0:T(1,128)S(1)}, u32[]{:S(2)}, u32[]{:S(2)}) async-start(s32[32,1,128]{2,1,0:T(1,128)} %reshape.157), calls=%async_computation | async-start | bytes 32768 | tf_op jit(solution)/shard_map/all_to_all | solution.py:82
  72.2 2.2 %all-gather.2.cloned.1.call-done = bf16[1024,1024]{1,0:T(8,128)(2,1)} async-done(((bf16[128,1024]{1,0:T(8,128)(2,1)}), bf16[1024,1024]{1,0:T(8,128)(2,1)}) %all-gather.2.cloned.1.call-update) | async-done | bytes 2097168 | tf_op jit(solution)/shard_map/all_gather | solution.py:57
  74.4 8.6 %scatter_custom_fusion.1 = bf16[2048,1024]{1,0:T(8,128)(2,1)} fusion(s32[1024]{0:T(1024)S(1)} %bitcast.49, bf16[1024,1024]{1,0:T(8,128)(2,1)} %all-gather.2.cloned.1.call-done, bf16[]{:T(256)} %constant.144.clone.1), kind=kCustom, calls=%fused_computation.27 | custom fusion | bytes 4194816 | tf_op jit(solution)/shard_map/scatter | solution.py:69
  82.9 9.7 %all-to-all-start.1 = ((bf16[32,64,1024]{2,1,0:T(8,128)(2,1)}), bf16[32,64,1024]{2,1,0:T(8,128)(2,1)}, u32[]{:S(2)}, u32[]{:S(2)}) async-start(bf16[32,64,1024]{2,1,0:T(8,128)(2,1)} %bitcast.36), calls=%async_computation.1 | async-start | bytes 8388608 | tf_op jit(solution)/shard_map/all_to_all | solution.py:75
  92.6 0.5 broadcast.140
  93.1 0.7 reduce.6
  94.3 92.6 %all-to-all-done.1 = bf16[32,64,1024]{2,1,0:T(8,128)(2,1)} async-done(((bf16[32,64,1024]{2,1,0:T(8,128)(2,1)}), bf16[32,64,1024]{2,1,0:T(8,128)(2,1)}, u32[]{:S(2)}, u32[]{:S(2)}) %all-to-all-start.1) | async-done | bytes 4194336 | tf_op jit(solution)/shard_map/all_to_all | solution.py:75
  186.9 4.0 %fusion.18 = f32[256]{0:T(256)S(1)} fusion(bf16[2048,1024]{1,0:T(8,128)(2,1)} %bitcast.15, s32[2048]{0:T(1024)S(1)} %bitcast.45, s32[2048]{0:T(1024)S(1)} %bitcast.44, s32[256]{0:T(256)S(1)} %bitcast.51, s32[256]{0:T(256)S(1)} %bitcast.50, pred[256]{0:T(512)(128)(4,1)S(1)} %compare_reduce_fusion, bf16[32,8,8,1024]{3,2,1,0:T(8,128)(2,1)} %bitcast.13, ...), kind=kOutput, calls=%fused_computation.30 | convolution fusion | flops 1076887296 | bytes 4738308 | tf_op jit(solution)/shard_map/dot_general | solution.py:24
  190.9 0.7 max_broadcast_in_dim.15
  191.6 7.5 %all-to-all-start.2 = ((f32[32,1,8]{2,1,0:T(1,128)}), f32[32,1,8]{2,1,0:T(1,128)S(1)}, u32[]{:S(2)}, u32[]{:S(2)}) async-start(f32[32,1,8]{2,1,0:T(1,128)} %bitcast.16), calls=%async_computation.2 | async-start | bytes 32768 | tf_op jit(solution)/shard_map/all_to_all | solution.py:103
  199.2 8.6 %all-to-all-done.2 = f32[32,1,8]{2,1,0:T(1,128)S(1)} async-done(((f32[32,1,8]{2,1,0:T(1,128)}), f32[32,1,8]{2,1,0:T(1,128)S(1)}, u32[]{:S(2)}, u32[]{:S(2)}) %all-to-all-start.2) | async-done | bytes 1056 | tf_op jit(solution)/shard_map/all_to_all | solution.py:103
  207.8 0.5 broadcast.139
  208.3 0.7 reduce.5
  209.1 1.3 gather_fusion
  210.4 0.5 bitcast_select_fusion
  (34 shorter events, 1.2 us)
Async XLA Ops:
  7.2 67.2 %all-gather.2.cloned.1.call-start = ((), (), s32[]{:S(2)}) async-start(), calls=%async_computation.3 | async-start | bytes 2359296 | tf_op jit(solution)/shard_map/all_gather | solution.py:57
  8.0 30.1 %copy-start = (bf16[1024,1024]{1,0:T(8,128)(2,1)S(1)}, bf16[1024,1024]{1,0:T(8,128)(2,1)}, u32[]{:S(2)}) copy-start(bf16[1024,1024]{1,0:T(8,128)(2,1)} %param.8) | copy-start | bytes 6291460
  8.0 30.1 %copy-start.1 = (s32[1,1024]{1,0:T(1,128)S(1)}, s32[1,1024]{1,0:T(1,128)}, u32[]{:S(2)}) copy-start(s32[1,1024]{1,0:T(1,128)} %param.9) | copy-start | bytes 12292
  8.0 30.1 %copy-start.3 = (f32[1024]{0:T(1024)S(1)}, f32[1024]{0:T(1024)}, u32[]{:S(2)}) copy-start(f32[1024]{0:T(1024)} %param.13) | copy-start | bytes 12292
  38.2 4.0 %copy-start.2 = (s32[128,1]{0,1:T(1,128)S(1)}, s32[128,1]{0,1:T(1,128)}, u32[]{:S(2)}) copy-start(s32[128,1]{0,1:T(1,128)} %param.14) | copy-start | bytes 1540
  38.2 4.4 %copy-start.4 = (s32[128]{0:T(128)S(1)}, s32[128]{0:T(128)}, u32[]{:S(2)}) copy-start(s32[128]{0:T(128)} %param.15) | copy-start | bytes 1540
  61.9 21.0 %all-to-all-start = ((s32[32,1,128]{2,1,0:T(1,128)}), s32[32,1,128]{2,1,0:T(1,128)S(1)}, u32[]{:S(2)}, u32[]{:S(2)}) async-start(s32[32,1,128]{2,1,0:T(1,128)} %reshape.157), calls=%async_computation | async-start | bytes 32768 | tf_op jit(solution)/shard_map/all_to_all | solution.py:82
  82.9 104.0 %all-to-all-start.1 = ((bf16[32,64,1024]{2,1,0:T(8,128)(2,1)}), bf16[32,64,1024]{2,1,0:T(8,128)(2,1)}, u32[]{:S(2)}, u32[]{:S(2)}) async-start(bf16[32,64,1024]{2,1,0:T(8,128)(2,1)} %bitcast.36), calls=%async_computation.1 | async-start | bytes 8388608 | tf_op jit(solution)/shard_map/all_to_all | solution.py:75
  191.6 16.2 %all-to-all-start.2 = ((f32[32,1,8]{2,1,0:T(1,128)}), f32[32,1,8]{2,1,0:T(1,128)S(1)}, u32[]{:S(2)}, u32[]{:S(2)}) async-start(f32[32,1,8]{2,1,0:T(1,128)} %bitcast.16), calls=%async_computation.2 | async-start | bytes 32768 | tf_op jit(solution)/shard_map/all_to_all | solution.py:103
Sparse Core Ops, SparseCore 0:
  42.3 32.0 all-gather.1
where the time goes:
time: 218 us
  waiting for transfers between devices  103 us (47%)
  matrix products  37.2 us (17%)
  starting transfers between devices  27.5 us (13%)
  local copies, waits for them, and re-layouts  16.8 us (8%)
  blocking collectives  14.5 us (7%)
  between operations  14.2 us (7%)
  other arithmetic  4.08 us (2%)
    all_to_all x1, waiting for transfers between devices, per_device(): lax.all_to_all(send_units.reshape(n_clu, n_grp * capacity, model_width),...  92.6 us
    dot_general x1, matrix products, encode(): jnp.dot(activated, w_out, preferred_element_type=jnp.float32)  30.1 us
    all_gather x1, blocking collectives, per_device(): lax.all_gather(doc_info, 'grp', axis=0, tiled=True)  14.5 us
    all_to_all x1, starting transfers between devices, per_device(): lax.all_to_all(send_meta.reshape(n_clu, n_grp * capacity, 2), 'clu', spli...  10.2 us
    all_to_all x1, starting transfers between devices, per_device(): lax.all_to_all(send_units.reshape(n_clu, n_grp * capacity, model_width),...  9.67 us
    all_to_all x1, waiting for transfers between devices, per_device(): lax.all_to_all(best_sim.reshape(n_clu, capacity), 'clu', split_axis=0, co...  8.64 us
    scatter x1, local copies, waits for them, and re-layouts, per_device(): send_units = jnp.zeros((n_clu * n_grp * capacity, model_width), jnp.bfloa...  8.55 us
    all_to_all x1, starting transfers between devices, per_device(): lax.all_to_all(best_sim.reshape(n_clu, capacity), 'clu', split_axis=0, co...  7.54 us
  transfers between devices with their start and end apart: 4, of which 3 were waited for; matrix products, arithmetic and copies ran while one was open for 7% of the time, Pallas kernels for 0%

commit v1 on v0

v1 whole, which is shorter than its diff:
```python
import jax
import jax.numpy as jnp
from jax import lax
from jax.sharding import PartitionSpec as P


def encode(token_block, segments, w_in, b_in, w_out, b_out, doc_count):
    pre_act = jnp.dot(token_block, w_in, preferred_element_type=jnp.float32) + b_in
    activated = jax.nn.gelu(pre_act, approximate=False).astype(jnp.bfloat16)
    layer_out = (
        token_block.astype(jnp.float32)
        + jnp.dot(activated, w_out, preferred_element_type=jnp.float32)
        + b_out
    ).astype(jnp.bfloat16)
    member = segments[None, :] == jnp.arange(doc_count, dtype=jnp.int32)[:, None]
    totals = jnp.dot(member.astype(jnp.bfloat16), layer_out, preferred_element_type=jnp.float32)
    counts = jnp.sum(member.astype(jnp.float32), axis=1, keepdims=True)
    mean_rows = totals / counts
    scale_inv = lax.rsqrt(jnp.sum(mean_rows * mean_rows, axis=1, keepdims=True) + 1e-06)
    return (mean_rows.astype(jnp.bfloat16), (mean_rows * scale_inv).astype(jnp.bfloat16))


def slot_ranks(owner_rank, n_clu):
    hits = (owner_rank[..., None] == jnp.arange(n_clu, dtype=jnp.int32)).astype(jnp.int32)
    before = jnp.cumsum(hits, axis=-2) - hits
    return jnp.sum(before * hits, axis=-1)


def per_device(tokens, segment_ids, w_in, b_in, w_out, b_out, owner_ids, sub_ids):
    n_clu = lax.axis_size("clu")
    n_grp = lax.axis_size("grp")
    doc_count = owner_ids.shape[0]
    model_width = tokens.shape[1]
    capacity = 8
    clu_index = lax.axis_index("clu")
    grp_index = lax.axis_index("grp")

    pooled, unit_rows = encode(tokens, segment_ids[0], w_in, b_in, w_out, b_out, doc_count)

    owner_rank = owner_ids[:, 0]
    slot_index = slot_ranks(owner_rank, n_clu)
    slot_place = owner_rank * capacity + slot_index
    key_code = sub_ids + 1
    lane = jnp.arange(128, dtype=jnp.int32)[None, :]
    meta_cols = jnp.where(
        lane == 0, key_code[:, None] // 64, jnp.where(lane == 1, key_code[:, None] % 64, 0)
    ).astype(jnp.bfloat16)
    rows = jnp.concatenate([unit_rows, meta_cols], axis=1)
    row_width = rows.shape[1]
    send_pick = (
        slot_place[None, :] == jnp.arange(n_clu * capacity, dtype=jnp.int32)[:, None]
    ).astype(jnp.bfloat16)
    send_rows = jnp.dot(send_pick, rows, preferred_element_type=jnp.float32).astype(jnp.bfloat16)
    own_rows = lax.all_to_all(
        send_rows.reshape(n_clu, capacity, row_width), "clu", split_axis=0, concat_axis=0,
        tiled=True,
    ).reshape(n_clu * capacity, row_width)
    all_rows = lax.all_gather(own_rows, "grp", axis=0, tiled=True)

    n_dev = n_clu * n_grp
    key = (
        all_rows[:, model_width].astype(jnp.int32) * 64
        + all_rows[:, model_width + 1].astype(jnp.int32)
        - 1
    )
    own_key = (
        own_rows[:, model_width].astype(jnp.int32) * 64
        + own_rows[:, model_width + 1].astype(jnp.int32)
        - 1
    )
    own_units = own_rows[:, :model_width]
    all_units = all_rows[:, :model_width]

    similar = lax.dot_general(
        own_units, all_units, (((1,), (1,)), ((), ())), preferred_element_type=jnp.float32
    )
    own_pos = grp_index * (n_clu * capacity) + jnp.arange(n_clu * capacity, dtype=jnp.int32)
    matched = (
        (own_key[:, None] == key[None, :])
        & (own_key[:, None] >= 0)
        & (own_pos[:, None] != jnp.arange(n_dev * capacity, dtype=jnp.int32)[None, :])
    )
    best_sim = jnp.max(jnp.where(matched, similar, -1.0), axis=1)
    returned = lax.all_to_all(
        best_sim.reshape(n_clu, capacity), "clu", split_axis=0, concat_axis=0, tiled=True
    ).reshape(n_clu * capacity)
    nearest = jnp.sum(
        jnp.where(
            slot_place[:, None] == jnp.arange(n_clu * capacity, dtype=jnp.int32)[None, :],
            returned[None, :],
            0.0,
        ),
        axis=1,
    )
    return (pooled, nearest)


def solution(mesh):
    in_specs = (
        P(("clu", "grp"), None),
        P(("clu", "grp"), None),
        P(),
        P(),
        P(),
        P(),
        P(("clu", "grp"), None),
        P(("clu", "grp")),
    )
    out_specs = (P(("clu", "grp"), None), P(("clu", "grp")))
    return jax.shard_map(
        per_device, mesh=mesh, in_specs=in_specs, out_specs=out_specs, check_vma=False
    )
```

time: 218 us -> 145 us (0.67)
  waiting for transfers between devices: 103 us -> 49.6 us
  starting transfers between devices: 27.5 us -> 9.57 us
  local copies, waits for them, and re-layouts: 16.8 us -> 2.41 us
  blocking collectives: 14.5 us -> 27 us
    all_to_all x2 -> x0, waiting for transfers between devices: 92.6 us -> none  [the longest x1 92.6 us: per_device(): lax.all_to_all(send_units.reshape(n_clu, n_grp * capacity, model_width),...]
    all_gather x1, waiting for transfers between devices: 2.2 us -> 40.9 us  [per_device(): all_rows = lax.all_gather(own_rows, 'grp', axis=0, tiled=True)]
    all_to_all x0 -> x1, blocking collectives: none -> 27 us  [per_device(): lax.all_to_all(send_rows.reshape(n_clu, capacity, row_width), 'clu', spli...]
    all_to_all x2 -> x0, starting transfers between devices: 19.9 us -> none  [the longest x1 10.2 us: per_device(): lax.all_to_all(send_meta.reshape(n_clu, n_grp * capacity, 2), 'clu', spli...]
    all_gather x1 -> x0, blocking collectives: 14.5 us -> none  [per_device(): lax.all_gather(doc_info, 'grp', axis=0, tiled=True)]
    scatter x2 -> x0, local copies, waits for them, and re-layouts: 11.9 us -> none  [the longest x1 8.55 us: per_device(): send_units = jnp.zeros((n_clu * n_grp * capacity, model_width), jnp.bfloa...]
  transfers between devices with their start and end apart: 4 -> 2, of which waited for: 3 -> 2; matrix products, arithmetic and copies ran while one was open for 7% -> 0% of each run, Pallas kernels for 0% -> 0%
where the time goes in v1:
time: 145 us
  waiting for transfers between devices  49.6 us (34%)
  matrix products  37.6 us (26%)
  blocking collectives  27 us (19%)
  between operations  14.2 us (10%)
  starting transfers between devices  9.57 us (7%)
  other arithmetic  4.77 us (3%)
  local copies, waits for them, and re-layouts  2.41 us (2%)
    all_gather x1, waiting for transfers between devices, per_device(): all_rows = lax.all_gather(own_rows, 'grp', axis=0, tiled=True)  40.9 us
    dot_general x1, matrix products, encode(): jnp.dot(activated, w_out, preferred_element_type=jnp.float32)  30.1 us
    all_to_all x1, blocking collectives, per_device(): lax.all_to_all(send_rows.reshape(n_clu, capacity, row_width), 'clu', spli...  27 us
    all_to_all x1, starting transfers between devices, per_device(): lax.all_to_all(best_sim.reshape(n_clu, capacity), 'clu', split_axis=0, co...  9.54 us
    all_to_all x1, waiting for transfers between devices, per_device(): lax.all_to_all(best_sim.reshape(n_clu, capacity), 'clu', split_axis=0, co...  8.64 us
    dot_general x1, matrix products, per_device(): lax.dot_general(own_units, all_units, (((1,), (1,)), ((), ())), preferred...  3.81 us
    dot_general x1, matrix products, encode(): jnp.dot(member.astype(jnp.bfloat16), layer_out, preferred_element_type=jn...  3.11 us
  transfers between devices with their start and end apart: 2, of which 2 were waited for; matrix products, arithmetic and copies ran while one was open for 0% of the time, Pallas kernels for 0%

profile of v1, /device:TPU:1, one launch (start us, length us, event | category | flops | bytes accessed | tf_op | source)
XLA Modules:
  0.0 145.1 jit_solution(5998165109606025520)
XLA Ops:
  7.2 0.0 all-gather.2.cloned.1.call-start
  7.2 0.8 convert_reduce_fusion
  8.1 30.1 %fusion.12 = f32[1024,1024]{1,0:T(8,128)} fusion(bf16[2048,1024]{1,0:T(8,128)(2,1)} %param.12, f32[2048]{0:T(1024)} %param.11, bf16[1024,1024]{1,0:T(8,128)(2,1)} %param.8, bf16[1024,2048]{1,0:T(8,128)(2,1)} %param.10), kind=kOutput, calls=%fused_computation.22 | convolution fusion | flops 8728346624 | bytes 14688256 | tf_op jit(solution)/shard_map/dot_general | solution.py:12
  38.2 3.1 %multiply_reduce_fusion = (f32[128]{0:T(128)S(1)}, f32[128,1024]{1,0:T(8,128)S(1)}) fusion(f32[128]{0:T(128)S(1)} %convert_reduce_fusion, f32[1024,1024]{1,0:T(8,128)} %fusion.12, bf16[1024,1024]{1,0:T(8,128)(2,1)S(1)} %copy-done, f32[1024]{0:T(1024)S(1)} %copy-done.2, s32[1024]{0:T(1024)S(1)} %bitcast.22), kind=kOutput, calls=%fused_computation.35 | convolution fusion | flops 273153920 | bytes 6824960 | tf_op jit(solution)/shard_map/dot_general | solution.py:16
  41.4 0.1 fusion.34
  41.5 0.2 reduce_window_sum.11
  41.7 0.2 select_reduce_fusion.1
  41.9 0.8 multiply_convert_fusion
  42.6 0.1 select_convert_fusion
  42.7 0.5 fusion.19
  43.3 27.0 %all_to_all.14 = bf16[32,8,1152]{2,1,0:T(8,128)(2,1)S(1)} all-to-all(bf16[32,8,1152]{2,1,0:T(8,128)(2,1)S(1)} %fusion.19), channel_id=1, replica_groups=mesh['clu'=32,'grp'=8] {'clu'}, dimensions={0} | all-to-all | bytes 1179648 | tf_op jit(solution)/shard_map/all_to_all | solution.py:54
  70.3 1.1 copy.13
  71.4 0.2 fusion.32
  71.6 0.2 compare_reduce_fusion
  71.8 40.9 %all-gather.2.cloned.1.call-done = bf16[2048,1152]{0,1:T(8,128)(2,1)} async-done(((bf16[256,1152]{0,1:T(8,128)(2,1)}), bf16[2048,1152]{0,1:T(8,128)(2,1)}) %all-gather.2.cloned.1.call-update) | async-done | bytes 4718608 | tf_op jit(solution)/shard_map/all_gather | solution.py:58
  112.7 0.9 fusion.36
  113.6 3.8 %fusion.23 = f32[256]{0:T(256)S(1)} fusion(bf16[2048,1152]{0,1:T(8,128)(2,1)} %all-gather.2.cloned.1.call-done, s32[256]{0:T(256)S(1)} %iota_add_fusion, s32[2048]{0:T(1024)S(1)} %bitcast.23, s32[256]{0:T(256)S(1)} %fusion.32, pred[256]{0:T(512)(128)(4,1)S(1)} %compare_reduce_fusion, bf16[256,1152]{1,0:T(8,128)(2,1)S(1)} %bitcast.20), kind=kOutput, calls=%fused_computation.31 | convolution fusion | flops 1076887296 | bytes 4730368 | tf_op jit(solution)/shard_map/dot_general | solution.py:74
  117.4 0.7 all_to_all.10
  118.1 9.5 %all-to-all-start.1 = ((f32[32,1,8]{2,1,0:T(1,128)}), f32[32,1,8]{2,1,0:T(1,128)S(1)}, u32[]{:S(2)}, u32[]{:S(2)}) async-start(f32[32,1,8]{2,1,0:T(1,128)} %bitcast.7), calls=%async_computation.1 | async-start | bytes 32768 | tf_op jit(solution)/shard_map/all_to_all | solution.py:84
  127.6 8.6 %all-to-all-done.1 = f32[32,1,8]{2,1,0:T(1,128)S(1)} async-done(((f32[32,1,8]{2,1,0:T(1,128)}), f32[32,1,8]{2,1,0:T(1,128)S(1)}, u32[]{:S(2)}, u32[]{:S(2)}) %all-to-all-start.1) | async-done | bytes 1056 | tf_op jit(solution)/shard_map/all_to_all | solution.py:84
  136.3 0.5 broadcast.98
  136.8 0.7 reduce.7
  137.5 0.1 broadcast_in_dim.78
  137.5 0.7 select_reduce_fusion
  (18 shorter events, 0.1 us)
Async XLA Ops:
  7.2 105.5 %all-gather.2.cloned.1.call-start = ((), (), s32[]{:S(2)}) async-start(), calls=%async_computation.2 | async-start | bytes 5308416 | tf_op jit(solution)/shard_map/all_gather | solution.py:58
  8.0 30.2 %copy-start = (bf16[1024,1024]{1,0:T(8,128)(2,1)S(1)}, bf16[1024,1024]{1,0:T(8,128)(2,1)}, u32[]{:S(2)}) copy-start(bf16[1024,1024]{1,0:T(8,128)(2,1)} %param.8) | copy-start | bytes 6291460
  8.1 30.2 %copy-start.1 = (s32[1,1024]{1,0:T(1,128)S(1)}, s32[1,1024]{1,0:T(1,128)}, u32[]{:S(2)}) copy-start(s32[1,1024]{1,0:T(1,128)} %param.9) | copy-start | bytes 12292
  8.1 30.2 %copy-start.2 = (f32[1024]{0:T(1024)S(1)}, f32[1024]{0:T(1024)}, u32[]{:S(2)}) copy-start(f32[1024]{0:T(1024)} %param.13) | copy-start | bytes 12292
  38.2 3.1 %copy-start.4 = (s32[128]{0:T(128)S(1)}, s32[128]{0:T(128)}, u32[]{:S(2)}) copy-start(s32[128]{0:T(128)} %param.15) | copy-start | bytes 1540
  38.2 3.2 %copy-start.3 = (s32[128,1]{0,1:T(1,128)S(1)}, s32[128,1]{0,1:T(1,128)}, u32[]{:S(2)}) copy-start(s32[128,1]{0,1:T(1,128)} %param.14) | copy-start | bytes 1540
  118.1 18.2 %all-to-all-start.1 = ((f32[32,1,8]{2,1,0:T(1,128)}), f32[32,1,8]{2,1,0:T(1,128)S(1)}, u32[]{:S(2)}, u32[]{:S(2)}) async-start(f32[32,1,8]{2,1,0:T(1,128)} %bitcast.7), calls=%async_computation.1 | async-start | bytes 32768 | tf_op jit(solution)/shard_map/all_to_all | solution.py:84
Sparse Core Ops, SparseCore 0:
  71.5 41.1 all-gather.1

commit v2 on v1

--- a/solution.py
+++ b/solution.py
@@ -24,6 +24,22 @@
     hits = (owner_rank[..., None] == jnp.arange(n_clu, dtype=jnp.int32)).astype(jnp.int32)
     before = jnp.cumsum(hits, axis=-2) - hits
     return jnp.sum(before * hits, axis=-1)
+
+
+def gather_grp(block):
+    n = lax.axis_size("grp")
+    chips = n // 2
+    core_swap = [(i, i ^ 1) for i in range(n)]
+    ring = [
+        (i, ((i // 2 + (1 if i % 2 == 0 else chips - 1)) % chips) * 2 + i % 2) for i in range(n)
+    ]
+    partner = lax.ppermute(block, "grp", core_swap)
+    pair = jnp.concatenate([block, partner], axis=0)
+    hop1 = lax.ppermute(pair, "grp", ring)
+    hop2 = lax.ppermute(hop1[: block.shape[0]], "grp", ring)
+    mine = jnp.concatenate([hop1, hop2], axis=0)
+    theirs = lax.ppermute(mine, "grp", core_swap)
+    return [block, partner, hop1, hop2, theirs]
 
 
 def per_device(tokens, segment_ids, w_in, b_in, w_out, b_out, owner_ids, sub_ids):
@@ -55,32 +71,31 @@
         send_rows.reshape(n_clu, capacity, row_width), "clu", split_axis=0, concat_axis=0,
         tiled=True,
     ).reshape(n_clu * capacity, row_width)
-    all_rows = lax.all_gather(own_rows, "grp", axis=0, tiled=True)
+    pieces = gather_grp(own_rows)
 
-    n_dev = n_clu * n_grp
-    key = (
-        all_rows[:, model_width].astype(jnp.int32) * 64
-        + all_rows[:, model_width + 1].astype(jnp.int32)
-        - 1
-    )
-    own_key = (
-        own_rows[:, model_width].astype(jnp.int32) * 64
-        + own_rows[:, model_width + 1].astype(jnp.int32)
-        - 1
-    )
+    def key_of(rows):
+        return (
+            rows[:, model_width].astype(jnp.int32) * 64
+            + rows[:, model_width + 1].astype(jnp.int32)
+            - 1
+        )
+
+    own_key = key_of(own_rows)
     own_units = own_rows[:, :model_width]
-    all_units = all_rows[:, :model_width]
-
-    similar = lax.dot_general(
-        own_units, all_units, (((1,), (1,)), ((), ())), preferred_element_type=jnp.float32
-    )
-    own_pos = grp_index * (n_clu * capacity) + jnp.arange(n_clu * capacity, dtype=jnp.int32)
-    matched = (
-        (own_key[:, None] == key[None, :])
-        & (own_key[:, None] >= 0)
-        & (own_pos[:, None] != jnp.arange(n_dev * capacity, dtype=jnp.int32)[None, :])
-    )
-    best_sim = jnp.max(jnp.where(matched, similar, -1.0), axis=1)
+    slots = n_clu * capacity
+    best_sim = jnp.full((slots,), -1.0, jnp.float32)
+    for number, piece in enumerate(pieces):
+        similar = lax.dot_general(
+            own_units, piece[:, :model_width], (((1,), (1,)), ((), ())),
+            preferred_element_type=jnp.float32,
+        )
+        matched = (own_key[:, None] == key_of(piece)[None, :]) & (own_key[:, None] >= 0)
+        if number == 0:
+            matched = matched & (
+                jnp.arange(slots, dtype=jnp.int32)[:, None]
+                != jnp.arange(piece.shape[0], dtype=jnp.int32)[None, :]
+            )
+        best_sim = jnp.maximum(best_sim, jnp.max(jnp.where(matched, similar, -1.0), axis=1))
     returned = lax.all_to_all(
         best_sim.reshape(n_clu, capacity), "clu", split_axis=0, concat_axis=0, tiled=True
     ).reshape(n_clu * capacity)

time: 145 us -> 120 us (0.83)
  waiting for transfers between devices: 49.6 us -> 31.8 us
  between operations: 14.2 us -> 0.82 us
  starting transfers between devices: 9.57 us -> 18.4 us
  matrix products: 37.6 us -> 36.1 us
    all_gather x1 -> x0, waiting for transfers between devices: 40.9 us -> none  [per_device(): all_rows = lax.all_gather(own_rows, 'grp', axis=0, tiled=True)]
    ppermute x0 -> x4, waiting for transfers between devices: none -> 23.2 us  [the longest x1 13.1 us: gather_grp(): hop1 = lax.ppermute(pair, 'grp', ring)]
    ppermute x0 -> x4, starting transfers between devices: none -> 12.7 us  [the longest x1 3.59 us: gather_grp(): partner = lax.ppermute(block, 'grp', core_swap)]
    all_to_all x1, starting transfers between devices: 9.54 us -> 5.67 us  [per_device(): lax.all_to_all(best_sim.reshape(n_clu, capacity), 'clu', split_axis=0, co...]
    dot_general x1 -> x5, matrix products: 3.81 us -> 2.36 us  [per_device(): lax.dot_general(own_units, piece[:, :model_width], (((1,), (1,)), ((), ()...]
  transfers between devices with their start and end apart: 2 -> 5, of which waited for: 2 -> 5; matrix products, arithmetic and copies ran while one was open for 0% -> 1% of each run, Pallas kernels for 0% -> 0%
where the time goes in v2:
time: 120 us
  matrix products  36.1 us (30%)
  waiting for transfers between devices  31.8 us (26%)
  blocking collectives  27 us (22%)
  starting transfers between devices  18.4 us (15%)
  other arithmetic  3.82 us (3%)
  local copies, waits for them, and re-layouts  1.61 us (1%)
    dot_general x1, matrix products, encode(): jnp.dot(activated, w_out, preferred_element_type=jnp.float32)  30.1 us
    all_to_all x1, blocking collectives, per_device(): lax.all_to_all(send_rows.reshape(n_clu, capacity, row_width), 'clu', spli...  27 us
    ppermute x1, waiting for transfers between devices, gather_grp(): hop1 = lax.ppermute(pair, 'grp', ring)  13.1 us
    all_to_all x1, waiting for transfers between devices, per_device(): lax.all_to_all(best_sim.reshape(n_clu, capacity), 'clu', split_axis=0, co...  8.64 us
    ppermute x1, waiting for transfers between devices, gather_grp(): hop2 = lax.ppermute(hop1[:block.shape[0]], 'grp', ring)  6.83 us
    all_to_all x1, starting transfers between devices, per_device(): lax.all_to_all(best_sim.reshape(n_clu, capacity), 'clu', split_axis=0, co...  5.67 us
    ppermute x1, starting transfers between devices, gather_grp(): partner = lax.ppermute(block, 'grp', core_swap)  3.59 us
    ppermute x1, starting transfers between devices, gather_grp(): hop2 = lax.ppermute(hop1[:block.shape[0]], 'grp', ring)  3.19 us
  transfers between devices with their start and end apart: 5, of which 5 were waited for; matrix products, arithmetic and copies ran while one was open for 1% of the time, Pallas kernels for 0%

profile of v2, /device:TPU:1, one launch (start us, length us, event | category | flops | bytes accessed | tf_op | source)
XLA Modules:
  0.0 119.6 jit_solution(6754972591642905541)
XLA Ops:
  0.6 0.8 convert_reduce_fusion
  1.5 30.1 %fusion.10 = f32[1024,1024]{1,0:T(8,128)} fusion(bf16[2048,1024]{1,0:T(8,128)(2,1)} %param.12, f32[2048]{0:T(1024)} %param.11, bf16[1024,1024]{1,0:T(8,128)(2,1)} %param.8, bf16[1024,2048]{1,0:T(8,128)(2,1)} %param.10), kind=kOutput, calls=%fused_computation.20 | convolution fusion | flops 8728346624 | bytes 14688256 | tf_op jit(solution)/shard_map/dot_general | solution.py:12
  31.6 3.1 %multiply_reduce_fusion = (f32[128]{0:T(128)S(1)}, f32[128,1024]{1,0:T(8,128)S(1)}) fusion(f32[128]{0:T(128)S(1)} %convert_reduce_fusion, f32[1024,1024]{1,0:T(8,128)} %fusion.10, bf16[1024,1024]{1,0:T(8,128)(2,1)S(1)} %copy-done, f32[1024]{0:T(1024)S(1)} %copy-done.2, s32[1024]{0:T(1024)S(1)} %bitcast.27), kind=kOutput, calls=%fused_computation.45 | convolution fusion | flops 273153920 | bytes 6824960 | tf_op jit(solution)/shard_map/dot_general | solution.py:16
  35.3 0.8 multiply_convert_fusion
  36.1 0.5 fusion.14
  36.6 27.0 %all_to_all.11 = bf16[32,8,1152]{2,1,0:T(8,128)(2,1)S(1)} all-to-all(bf16[32,8,1152]{2,1,0:T(8,128)(2,1)S(1)} %fusion.14), channel_id=1, replica_groups=mesh['clu'=32,'grp'=8] {'clu'}, dimensions={0} | all-to-all | bytes 1179648 | tf_op jit(solution)/shard_map/all_to_all | solution.py:70
  63.9 3.6 %collective-permute-start = (bf16[256,1152]{0,1:T(8,128)(2,1)S(1)}, bf16[256,1152]{0,1:T(8,128)(2,1)S(1)}, u32[]{:S(2)}, u32[]{:S(2)}) collective-permute-start(bf16[256,1152]{0,1:T(8,128)(2,1)S(1)} %copy.13), channel_id=1, source_target_pairs={{0,1},{1,0},{2,3},{3,2},{4,5},{5,4},{6,7},{7,6},{8,9},{9,8},{10,11... | collective-permute-start | bytes 1769480 | tf_op jit(solution)/shard_map/ppermute | solution.py:36
  67.5 1.6 %collective-permute-done = bf16[256,1152]{0,1:T(8,128)(2,1)S(1)} collective-permute-done((bf16[256,1152]{0,1:T(8,128)(2,1)S(1)}, bf16[256,1152]{0,1:T(8,128)(2,1)S(1)}, u32[]{:S(2)}, u32[]{:S(2)}) %collective-permute-start) | collective-permute-done | bytes 589856 | tf_op jit(solution)/shard_map/ppermute | solution.py:36
  69.3 2.8 %collective-permute-start.1 = (bf16[512,1152]{0,1:T(8,128)(2,1)S(1)}, bf16[512,1152]{0,1:T(8,128)(2,1)S(1)}, u32[]{:S(2)}, u32[]{:S(2)}) collective-permute-start(bf16[512,1152]{0,1:T(8,128)(2,1)S(1)} %pad_maximum_fusion.1), channel_id=1, source_target_pairs={{0,2},{1,7},{2,4},{3,1},{4,6},{5,3},{6,0},{7,5},{8,10},{9,15},{10,... | collective-permute-start | bytes 3538952 | tf_op jit(solution)/shard_map/ppermute | solution.py:38
  72.1 13.1 %collective-permute-done.1 = bf16[512,1152]{0,1:T(8,128)(2,1)S(1)} collective-permute-done((bf16[512,1152]{0,1:T(8,128)(2,1)S(1)}, bf16[512,1152]{0,1:T(8,128)(2,1)S(1)}, u32[]{:S(2)}, u32[]{:S(2)}) %collective-permute-start.1) | collective-permute-done | bytes 1179680 | tf_op jit(solution)/shard_map/ppermute | solution.py:38
  85.3 3.2 %collective-permute-start.2 = (bf16[256,1152]{0,1:T(8,128)(2,1)S(1)}, bf16[256,1152]{0,1:T(8,128)(2,1)S(1)}, u32[]{:S(2)}, u32[]{:S(2)}) collective-permute-start(bf16[256,1152]{0,1:T(8,128)(2,1)S(1)} %slice.76), channel_id=1, source_target_pairs={{0,2},{1,7},{2,4},{3,1},{4,6},{5,3},{6,0},{7,5},{8,10},{9,15},{10,... | collective-permute-start | bytes 1769480 | tf_op jit(solution)/shard_map/ppermute | solution.py:39
  88.5 6.8 %collective-permute-done.2 = bf16[256,1152]{0,1:T(8,128)(2,1)S(1)} collective-permute-done((bf16[256,1152]{0,1:T(8,128)(2,1)S(1)}, bf16[256,1152]{0,1:T(8,128)(2,1)S(1)}, u32[]{:S(2)}, u32[]{:S(2)}) %collective-permute-start.2) | collective-permute-done | bytes 589856 | tf_op jit(solution)/shard_map/ppermute | solution.py:39
  95.4 3.1 %collective-permute-start.3 = (bf16[768,1152]{0,1:T(8,128)(2,1)S(1)}, bf16[768,1152]{0,1:T(8,128)(2,1)S(1)}, u32[]{:S(2)}, u32[]{:S(2)}) collective-permute-start(bf16[768,1152]{0,1:T(8,128)(2,1)S(1)} %pad_maximum_fusion), channel_id=1, source_target_pairs={{0,1},{1,0},{2,3},{3,2},{4,5},{5,4},{6,7},{7,6},{8,9},{9,8},{10,11... | collective-permute-start | bytes 5308424 | tf_op jit(solution)/shard_map/ppermute | solution.py:41
  98.9 0.4 fusion.28
  99.4 0.5 fusion.26
  99.9 0.4 fusion.29
  100.3 1.6 %collective-permute-done.3 = bf16[768,1152]{0,1:T(8,128)(2,1)S(1)} collective-permute-done((bf16[768,1152]{0,1:T(8,128)(2,1)S(1)}, bf16[768,1152]{0,1:T(8,128)(2,1)S(1)}, u32[]{:S(2)}, u32[]{:S(2)}) %collective-permute-start.3) | collective-permute-done | bytes 1769504 | tf_op jit(solution)/shard_map/ppermute | solution.py:41
  101.9 0.7 fusion.22
  102.6 0.7 reshape.232
  103.3 5.7 %all-to-all-start.1 = ((f32[32,1,8]{2,1,0:T(1,128)}), f32[32,1,8]{2,1,0:T(1,128)S(1)}, u32[]{:S(2)}, u32[]{:S(2)}) async-start(f32[32,1,8]{2,1,0:T(1,128)} %bitcast.10), calls=%async_computation.1 | async-start | bytes 32768 | tf_op jit(solution)/shard_map/all_to_all | solution.py:99
  109.0 8.6 %all-to-all-done.1 = f32[32,1,8]{2,1,0:T(1,128)S(1)} async-done(((f32[32,1,8]{2,1,0:T(1,128)}), f32[32,1,8]{2,1,0:T(1,128)S(1)}, u32[]{:S(2)}, u32[]{:S(2)}) %all-to-all-start.1) | async-done | bytes 1056 | tf_op jit(solution)/shard_map/all_to_all | solution.py:99
  117.6 0.5 broadcast.169
  118.1 0.7 reduce.7
  118.9 0.7 select_reduce_fusion
  (32 shorter events, 1.6 us)
Async XLA Ops:
  1.5 30.1 %copy-start = (bf16[1024,1024]{1,0:T(8,128)(2,1)S(1)}, bf16[1024,1024]{1,0:T(8,128)(2,1)}, u32[]{:S(2)}) copy-start(bf16[1024,1024]{1,0:T(8,128)(2,1)} %param.8) | copy-start | bytes 6291460
  1.5 30.1 %copy-start.1 = (s32[1,1024]{1,0:T(1,128)S(1)}, s32[1,1024]{1,0:T(1,128)}, u32[]{:S(2)}) copy-start(s32[1,1024]{1,0:T(1,128)} %param.9) | copy-start | bytes 12292
  1.5 30.1 %copy-start.2 = (f32[1024]{0:T(1024)S(1)}, f32[1024]{0:T(1024)}, u32[]{:S(2)}) copy-start(f32[1024]{0:T(1024)} %param.13) | copy-start | bytes 12292
  31.6 3.1 %copy-start.4 = (s32[128]{0:T(128)S(1)}, s32[128]{0:T(128)}, u32[]{:S(2)}) copy-start(s32[128]{0:T(128)} %param.15) | copy-start | bytes 1540
  31.6 3.2 %copy-start.3 = (s32[128,1]{0,1:T(1,128)S(1)}, s32[128,1]{0,1:T(1,128)}, u32[]{:S(2)}) copy-start(s32[128,1]{0,1:T(1,128)} %param.14) | copy-start | bytes 1540
  63.9 5.2 %collective-permute-start = (bf16[256,1152]{0,1:T(8,128)(2,1)S(1)}, bf16[256,1152]{0,1:T(8,128)(2,1)S(1)}, u32[]{:S(2)}, u32[]{:S(2)}) collective-permute-start(bf16[256,1152]{0,1:T(8,128)(2,1)S(1)} %copy.13), channel_id=1, source_target_pairs={{0,1},{1,0},{2,3},{3,2},{4,5},{5,4},{6,7},{7,6},{8,9},{9,8},{10,11... | collective-permute-start | bytes 1769480 | tf_op jit(solution)/shard_map/ppermute | solution.py:36
  69.3 16.0 %collective-permute-start.1 = (bf16[512,1152]{0,1:T(8,128)(2,1)S(1)}, bf16[512,1152]{0,1:T(8,128)(2,1)S(1)}, u32[]{:S(2)}, u32[]{:S(2)}) collective-permute-start(bf16[512,1152]{0,1:T(8,128)(2,1)S(1)} %pad_maximum_fusion.1), channel_id=1, source_target_pairs={{0,2},{1,7},{2,4},{3,1},{4,6},{5,3},{6,0},{7,5},{8,10},{9,15},{10,... | collective-permute-start | bytes 3538952 | tf_op jit(solution)/shard_map/ppermute | solution.py:38
  85.3 10.0 %collective-permute-start.2 = (bf16[256,1152]{0,1:T(8,128)(2,1)S(1)}, bf16[256,1152]{0,1:T(8,128)(2,1)S(1)}, u32[]{:S(2)}, u32[]{:S(2)}) collective-permute-start(bf16[256,1152]{0,1:T(8,128)(2,1)S(1)} %slice.76), channel_id=1, source_target_pairs={{0,2},{1,7},{2,4},{3,1},{4,6},{5,3},{6,0},{7,5},{8,10},{9,15},{10,... | collective-permute-start | bytes 1769480 | tf_op jit(solution)/shard_map/ppermute | solution.py:39
  95.4 6.5 %collective-permute-start.3 = (bf16[768,1152]{0,1:T(8,128)(2,1)S(1)}, bf16[768,1152]{0,1:T(8,128)(2,1)S(1)}, u32[]{:S(2)}, u32[]{:S(2)}) collective-permute-start(bf16[768,1152]{0,1:T(8,128)(2,1)S(1)} %pad_maximum_fusion), channel_id=1, source_target_pairs={{0,1},{1,0},{2,3},{3,2},{4,5},{5,4},{6,7},{7,6},{8,9},{9,8},{10,11... | collective-permute-start | bytes 5308424 | tf_op jit(solution)/shard_map/ppermute | solution.py:41
  103.3 14.3 %all-to-all-start.1 = ((f32[32,1,8]{2,1,0:T(1,128)}), f32[32,1,8]{2,1,0:T(1,128)S(1)}, u32[]{:S(2)}, u32[]{:S(2)}) async-start(f32[32,1,8]{2,1,0:T(1,128)} %bitcast.10), calls=%async_computation.1 | async-start | bytes 32768 | tf_op jit(solution)/shard_map/all_to_all | solution.py:99

commit v3 on v2

--- a/solution.py
+++ b/solution.py
@@ -1,19 +1,68 @@
+import functools
+
 import jax
 import jax.numpy as jnp
 from jax import lax
+from jax.experimental import pallas as pl
+from jax.experimental.pallas import tpu as pltpu
 from jax.sharding import PartitionSpec as P
 
 
+def encode_kernel(chunk, seg_ref, x_ref, wi_ref, bi_ref, wo_ref, bo_ref, tot_ref):
+    step = pl.program_id(0)
+    x = x_ref[...]
+    ff = wi_ref.shape[1]
+    acc = None
+    for k in range(ff // chunk):
+        part = slice(k * chunk, (k + 1) * chunk)
+        pre_act = jnp.dot(x, wi_ref[:, part], preferred_element_type=jnp.float32) + bi_ref[:, part]
+        activated = (pre_act * 0.5 * (1.0 + lax.erf(pre_act * 0.7071067811865476))).astype(
+            jnp.bfloat16
+        )
+        term = jnp.dot(activated, wo_ref[part, :], preferred_element_type=jnp.float32)
+        acc = term if acc is None else acc + term
+    layer_out = (x.astype(jnp.float32) + acc + bo_ref[...]).astype(jnp.bfloat16)
+    docs = tot_ref.shape[0]
+    member = (
+        seg_ref[...] == lax.broadcasted_iota(jnp.int32, (docs, seg_ref.shape[1]), 0)
+    ).astype(jnp.bfloat16)
+    part_totals = jnp.dot(member, layer_out, preferred_element_type=jnp.float32)
+
+    @pl.when(step == 0)
+    def _():
+        tot_ref[...] = part_totals
+
+    @pl.when(step != 0)
+    def _():
+        tot_ref[...] += part_totals
+
+
 def encode(token_block, segments, w_in, b_in, w_out, b_out, doc_count):
-    pre_act = jnp.dot(token_block, w_in, preferred_element_type=jnp.float32) + b_in
-    activated = jax.nn.gelu(pre_act, approximate=False).astype(jnp.bfloat16)
-    layer_out = (
-        token_block.astype(jnp.float32)
-        + jnp.dot(activated, w_out, preferred_element_type=jnp.float32)
-        + b_out
-    ).astype(jnp.bfloat16)
+    rows, width = token_block.shape
+    ff = w_in.shape[1]
+    tile = 512
+    flops = 4 * rows * width * ff + 2 * doc_count * rows * width
+    totals = pl.pallas_call(
+        functools.partial(encode_kernel, 1024),
+        out_shape=jax.ShapeDtypeStruct((doc_count, width), jnp.float32),
+        grid=(rows // tile,),
+        in_specs=[
+            pl.BlockSpec((1, tile), lambda i: (0, i)),
+            pl.BlockSpec((tile, width), lambda i: (i, 0)),
+            pl.BlockSpec((width, ff), lambda i: (0, 0)),
+            pl.BlockSpec((1, ff), lambda i: (0, 0)),
+            pl.BlockSpec((ff, width), lambda i: (0, 0)),
+            pl.BlockSpec((1, width), lambda i: (0, 0)),
+        ],
+        out_specs=pl.BlockSpec((doc_count, width), lambda i: (0, 0)),
+        compiler_params=pltpu.CompilerParams(
+            dimension_semantics=("arbitrary",), vmem_limit_bytes=60 * 1024 * 1024
+        ),
+        cost_estimate=pl.CostEstimate(
+            flops=flops, transcendentals=rows * ff, bytes_accessed=2 * rows * width + 8 * width * ff
+        ),
+    )(segments.reshape(1, rows), token_block, w_in, b_in.reshape(1, ff), w_out, b_out.reshape(1, width))
     member = segments[None, :] == jnp.arange(doc_count, dtype=jnp.int32)[:, None]
-    totals = jnp.dot(member.astype(jnp.bfloat16), layer_out, preferred_element_type=jnp.float32)
     counts = jnp.sum(member.astype(jnp.float32), axis=1, keepdims=True)
     mean_rows = totals / counts
     scale_inv = lax.rsqrt(jnp.sum(mean_rows * mean_rows, axis=1, keepdims=True) + 1e-06)

time: 120 us -> 103 us (0.86)
  matrix products: 36.1 us -> 2.65 us
  Pallas kernels: 0 us -> 14.2 us
  other arithmetic: 3.82 us -> 6.19 us
    dot_general x2 -> x0, matrix products: 33.2 us -> none  [the longest x1 30.1 us: encode(): jnp.dot(activated, w_out, preferred_element_type=jnp.float32)]
    pallas_call x0 -> x1, Pallas kernels: none -> 14.2 us  [encode(): pl.pallas_call(functools.partial(encode_kernel, 1024), out_shape=jax.Shap...]
    reduce_sum x0 -> x1, other arithmetic: none -> 1.24 us  [encode(): jnp.sum(mean_rows * mean_rows, axis=1, keepdims=True) + 1e-06]
  transfers between devices with their start and end apart: 5 -> 5, of which waited for: 5 -> 5; matrix products, arithmetic and copies ran while one was open for 1% -> 2% of each run, Pallas kernels for 0% -> 0%
where the time goes in v3:
time: 103 us
  waiting for transfers between devices  31.8 us (31%)
  blocking collectives  27.1 us (26%)
  starting transfers between devices  18.4 us (18%)
  Pallas kernels  14.2 us (14%)
  other arithmetic  6.19 us (6%)
  matrix products  2.65 us (3%)
  local copies, waits for them, and re-layouts  1.58 us (2%)
    all_to_all x1, blocking collectives, per_device(): lax.all_to_all(send_rows.reshape(n_clu, capacity, row_width), 'clu', spli...  27.1 us
    pallas_call x1, Pallas kernels, encode(): pl.pallas_call(functools.partial(encode_kernel, 1024), out_shape=jax.Shap...  14.2 us
    ppermute x1, waiting for transfers between devices, gather_grp(): hop1 = lax.ppermute(pair, 'grp', ring)  13.1 us
    all_to_all x1, waiting for transfers between devices, per_device(): lax.all_to_all(best_sim.reshape(n_clu, capacity), 'clu', split_axis=0, co...  8.64 us
    ppermute x1, waiting for transfers between devices, gather_grp(): hop2 = lax.ppermute(hop1[:block.shape[0]], 'grp', ring)  6.83 us
    all_to_all x1, starting transfers between devices, per_device(): lax.all_to_all(best_sim.reshape(n_clu, capacity), 'clu', split_axis=0, co...  5.68 us
    ppermute x1, starting transfers between devices, gather_grp(): partner = lax.ppermute(block, 'grp', core_swap)  3.56 us
    ppermute x1, starting transfers between devices, gather_grp(): hop2 = lax.ppermute(hop1[:block.shape[0]], 'grp', ring)  3.19 us
  transfers between devices with their start and end apart: 5, of which 5 were waited for; matrix products, arithmetic and copies ran while one was open for 2% of the time, Pallas kernels for 0%

profile of v3, /device:TPU:1, one launch (start us, length us, event | category | flops | bytes accessed | tf_op | source)
XLA Modules:
  0.0 102.6 jit_solution(51005565205491055)
XLA Ops:
  0.6 0.8 convert_reduce_fusion
  1.5 14.2 %shard_map.95 = f32[128,1024]{1,0:T(8,128)} custom-call(s32[1,1024]{1,0:T(1,128)} %seg_ref.1, bf16[1024,1024]{1,0:T(8,128)(2,1)} %x_ref.1, bf16[1024,2048]{1,0:T(8,128)(2,1)} %wi_ref.1, f32[1,2048]{1,0:T(1,128)} %bitcast.36, bf16[2048,1024]{1,0:T(8,128)(2,1)} %wo_ref.1, f32[1,1024]{1,0:T(1,128)} %bitcast.37), custom_call_target="tpu_custom_call" | custom-call | flops 8858370048 | bytes 18874368 | tf_op jit(solution)/shard_map/pallas_call | solution.py:45
  15.6 1.2 %multiply_reduce_fusion = f32[128]{0:T(128)S(1)} fusion(f32[128,1024]{1,0:T(8,128)} %shard_map.95, f32[128]{0:T(128)S(1)} %convert_reduce_fusion), kind=kLoop, calls=%fused_computation.20 | loop fusion | flops 393088 | bytes 525312 | tf_op jit(solution)/shard_map/reduce_sum | solution.py:68
  16.9 1.9 %multiply_convert_fusion = (bf16[128,1024]{1,0:T(8,128)(2,1)S(1)}, bf16[128,1024]{1,0:T(8,128)(2,1)}) fusion(f32[128]{0:T(128)S(1)} %add_rsqrt_fusion, f32[128,1024]{1,0:T(8,128)} %shard_map.95, f32[128]{0:T(128)S(1)} %convert_reduce_fusion), kind=kLoop, calls=%fused_computation.19 | loop fusion | flops 524288 | bytes 1049600 | tf_op jit(solution)/shard_map/convert_element_type | solution.py:69
  19.7 27.1 %all_to_all.11 = bf16[32,8,1152]{2,1,0:T(8,128)(2,1)S(1)} all-to-all(bf16[32,8,1152]{2,1,0:T(8,128)(2,1)S(1)} %fusion), channel_id=1, replica_groups=mesh['clu'=32,'grp'=8] {'clu'}, dimensions={0} | all-to-all | bytes 1179648 | tf_op jit(solution)/shard_map/all_to_all | solution.py:119
  47.0 3.6 %collective-permute-start = (bf16[256,1152]{0,1:T(8,128)(2,1)S(1)}, bf16[256,1152]{0,1:T(8,128)(2,1)S(1)}, u32[]{:S(2)}, u32[]{:S(2)}) collective-permute-start(bf16[256,1152]{0,1:T(8,128)(2,1)S(1)} %copy.13), channel_id=1, source_target_pairs={{0,1},{1,0},{2,3},{3,2},{4,5},{5,4},{6,7},{7,6},{8,9},{9,8},{10,11... | collective-permute-start | bytes 1769480 | tf_op jit(solution)/shard_map/ppermute | solution.py:85
  50.5 1.6 %collective-permute-done = bf16[256,1152]{0,1:T(8,128)(2,1)S(1)} collective-permute-done((bf16[256,1152]{0,1:T(8,128)(2,1)S(1)}, bf16[256,1152]{0,1:T(8,128)(2,1)S(1)}, u32[]{:S(2)}, u32[]{:S(2)}) %collective-permute-start) | collective-permute-done | bytes 589856 | tf_op jit(solution)/shard_map/ppermute | solution.py:85
  52.3 2.8 %collective-permute-start.1 = (bf16[512,1152]{0,1:T(8,128)(2,1)S(1)}, bf16[512,1152]{0,1:T(8,128)(2,1)S(1)}, u32[]{:S(2)}, u32[]{:S(2)}) collective-permute-start(bf16[512,1152]{0,1:T(8,128)(2,1)S(1)} %pad_maximum_fusion.1), channel_id=1, source_target_pairs={{0,2},{1,7},{2,4},{3,1},{4,6},{5,3},{6,0},{7,5},{8,10},{9,15},{10,... | collective-permute-start | bytes 3538952 | tf_op jit(solution)/shard_map/ppermute | solution.py:87
  55.1 13.1 %collective-permute-done.1 = bf16[512,1152]{0,1:T(8,128)(2,1)S(1)} collective-permute-done((bf16[512,1152]{0,1:T(8,128)(2,1)S(1)}, bf16[512,1152]{0,1:T(8,128)(2,1)S(1)}, u32[]{:S(2)}, u32[]{:S(2)}) %collective-permute-start.1) | collective-permute-done | bytes 1179680 | tf_op jit(solution)/shard_map/ppermute | solution.py:87
  68.3 3.2 %collective-permute-start.2 = (bf16[256,1152]{0,1:T(8,128)(2,1)S(1)}, bf16[256,1152]{0,1:T(8,128)(2,1)S(1)}, u32[]{:S(2)}, u32[]{:S(2)}) collective-permute-start(bf16[256,1152]{0,1:T(8,128)(2,1)S(1)} %slice.76), channel_id=1, source_target_pairs={{0,2},{1,7},{2,4},{3,1},{4,6},{5,3},{6,0},{7,5},{8,10},{9,15},{10,... | collective-permute-start | bytes 1769480 | tf_op jit(solution)/shard_map/ppermute | solution.py:88
  71.5 6.8 %collective-permute-done.2 = bf16[256,1152]{0,1:T(8,128)(2,1)S(1)} collective-permute-done((bf16[256,1152]{0,1:T(8,128)(2,1)S(1)}, bf16[256,1152]{0,1:T(8,128)(2,1)S(1)}, u32[]{:S(2)}, u32[]{:S(2)}) %collective-permute-start.2) | collective-permute-done | bytes 589856 | tf_op jit(solution)/shard_map/ppermute | solution.py:88
  78.4 3.1 %collective-permute-start.3 = (bf16[768,1152]{0,1:T(8,128)(2,1)S(1)}, bf16[768,1152]{0,1:T(8,128)(2,1)S(1)}, u32[]{:S(2)}, u32[]{:S(2)}) collective-permute-start(bf16[768,1152]{0,1:T(8,128)(2,1)S(1)} %pad_maximum_fusion), channel_id=1, source_target_pairs={{0,1},{1,0},{2,3},{3,2},{4,5},{5,4},{6,7},{7,6},{8,9},{9,8},{10,11... | collective-permute-start | bytes 5308424 | tf_op jit(solution)/shard_map/ppermute | solution.py:90
  81.6 0.3 fusion.10
  82.0 0.4 fusion.11
  82.4 0.5 fusion.9
  82.9 0.4 fusion.12
  83.3 1.6 %collective-permute-done.3 = bf16[768,1152]{0,1:T(8,128)(2,1)S(1)} collective-permute-done((bf16[768,1152]{0,1:T(8,128)(2,1)S(1)}, bf16[768,1152]{0,1:T(8,128)(2,1)S(1)}, u32[]{:S(2)}, u32[]{:S(2)}) %collective-permute-start.3) | collective-permute-done | bytes 1769504 | tf_op jit(solution)/shard_map/ppermute | solution.py:90
  84.9 0.7 fusion.6
  85.6 0.7 reshape.238
  86.3 5.7 %all-to-all-start.1 = ((f32[32,1,8]{2,1,0:T(1,128)}), f32[32,1,8]{2,1,0:T(1,128)S(1)}, u32[]{:S(2)}, u32[]{:S(2)}) async-start(f32[32,1,8]{2,1,0:T(1,128)} %bitcast.12), calls=%async_computation.1 | async-start | bytes 32768 | tf_op jit(solution)/shard_map/all_to_all | solution.py:148
  92.0 8.6 %all-to-all-done.1 = f32[32,1,8]{2,1,0:T(1,128)S(1)} async-done(((f32[32,1,8]{2,1,0:T(1,128)}), f32[32,1,8]{2,1,0:T(1,128)S(1)}, u32[]{:S(2)}, u32[]{:S(2)}) %all-to-all-start.1) | async-done | bytes 1056 | tf_op jit(solution)/shard_map/all_to_all | solution.py:148
  100.6 0.5 broadcast.161
  101.2 0.7 reduce.7
  101.9 0.7 select_reduce_fusion
  (26 shorter events, 1.5 us)
Async XLA Ops:
  1.5 17.3 %copy-start.1 = (s32[128]{0:T(128)S(1)}, s32[128]{0:T(128)}, u32[]{:S(2)}) copy-start(s32[128]{0:T(128)} %param.15) | copy-start | bytes 1540
  1.5 17.3 %copy-start = (s32[128,1]{0,1:T(1,128)S(1)}, s32[128,1]{0,1:T(1,128)}, u32[]{:S(2)}) copy-start(s32[128,1]{0,1:T(1,128)} %param.14) | copy-start | bytes 1540
  47.0 5.2 %collective-permute-start = (bf16[256,1152]{0,1:T(8,128)(2,1)S(1)}, bf16[256,1152]{0,1:T(8,128)(2,1)S(1)}, u32[]{:S(2)}, u32[]{:S(2)}) collective-permute-start(bf16[256,1152]{0,1:T(8,128)(2,1)S(1)} %copy.13), channel_id=1, source_target_pairs={{0,1},{1,0},{2,3},{3,2},{4,5},{5,4},{6,7},{7,6},{8,9},{9,8},{10,11... | collective-permute-start | bytes 1769480 | tf_op jit(solution)/shard_map/ppermute | solution.py:85
  52.3 16.0 %collective-permute-start.1 = (bf16[512,1152]{0,1:T(8,128)(2,1)S(1)}, bf16[512,1152]{0,1:T(8,128)(2,1)S(1)}, u32[]{:S(2)}, u32[]{:S(2)}) collective-permute-start(bf16[512,1152]{0,1:T(8,128)(2,1)S(1)} %pad_maximum_fusion.1), channel_id=1, source_target_pairs={{0,2},{1,7},{2,4},{3,1},{4,6},{5,3},{6,0},{7,5},{8,10},{9,15},{10,... | collective-permute-start | bytes 3538952 | tf_op jit(solution)/shard_map/ppermute | solution.py:87
  68.3 10.0 %collective-permute-start.2 = (bf16[256,1152]{0,1:T(8,128)(2,1)S(1)}, bf16[256,1152]{0,1:T(8,128)(2,1)S(1)}, u32[]{:S(2)}, u32[]{:S(2)}) collective-permute-start(bf16[256,1152]{0,1:T(8,128)(2,1)S(1)} %slice.76), channel_id=1, source_target_pairs={{0,2},{1,7},{2,4},{3,1},{4,6},{5,3},{6,0},{7,5},{8,10},{9,15},{10,... | collective-permute-start | bytes 1769480 | tf_op jit(solution)/shard_map/ppermute | solution.py:88
  78.4 6.5 %collective-permute-start.3 = (bf16[768,1152]{0,1:T(8,128)(2,1)S(1)}, bf16[768,1152]{0,1:T(8,128)(2,1)S(1)}, u32[]{:S(2)}, u32[]{:S(2)}) collective-permute-start(bf16[768,1152]{0,1:T(8,128)(2,1)S(1)} %pad_maximum_fusion), channel_id=1, source_target_pairs={{0,1},{1,0},{2,3},{3,2},{4,5},{5,4},{6,7},{7,6},{8,9},{9,8},{10,11... | collective-permute-start | bytes 5308424 | tf_op jit(solution)/shard_map/ppermute | solution.py:90
  86.3 14.3 %all-to-all-start.1 = ((f32[32,1,8]{2,1,0:T(1,128)}), f32[32,1,8]{2,1,0:T(1,128)S(1)}, u32[]{:S(2)}, u32[]{:S(2)}) async-start(f32[32,1,8]{2,1,0:T(1,128)} %bitcast.12), calls=%async_computation.1 | async-start | bytes 32768 | tf_op jit(solution)/shard_map/all_to_all | solution.py:148
